TPU v7x, 256 devices: a whole 4x4x8 slice. The times are simulated.
256 devices in a mesh: row: 2 (over core), col: 2 (over x_lo), rhs: 64 (over z, y, x_hi).
Axes of the slice: x: 4 (x_hi: 2, x_lo: 2; x = x_hi * 2 + x_lo), y: 4, z: 8, core: 2. Of those that a mesh axis runs over, the one named last changes fastest.
Arguments:
- front: bfloat16 [4096, 4096], P(('row', 'rhs'), 'col'), as said below
- anc_weight: bfloat16 [1024, 4096], P(('row', 'rhs'), 'col'), may hold values from -0.1875 to 0.1875
- solved: bfloat16 [2048, 8192], P(('row', 'col'), 'rhs'), may hold values from -6 to 6
- owners: int32 [8], replicated, may hold values from 0 to 3, as said below
- indices: int32 [8, 128], replicated, may hold values from 0 to 511
- counts: int32 [8], replicated, may hold values from 64 to 128, as said below
- rhs_side: bfloat16 [4096, 8192], P('row', 'rhs'), may hold values from -6 to 6
Outputs:
- solution: bfloat16 [4096, 8192], P('row', 'rhs')
Inputs may be any that keep to these rules, and one draw needn't show every extreme that they name: `front`: zero above the diagonal; diagonal entries 1 or more. The 4 tiles of each aligned block of 4 tiles have 4 different owners, numbered row index times 2 plus col index. `counts`: rows at or past a tile's count are padding.
All inputs are finite; a program needn't handle non-finite values.
Results may differ from a plain program's by a relative error of at most 0.0038.
Values may be sent and summed in bfloat16 or wider, within the bound.
No kernel may reach another device: no remote copies, remote signals or barrier semaphores. Data moves between devices by JAX's collectives and lax.ppermute only.
A program may use at most 128 MiB of HBM per device.

v0:
```python
import jax
import jax.numpy as jnp
from jax import lax
from jax.sharding import PartitionSpec as P

BLOCK = 128
HIGH = lax.Precision.HIGHEST


def split_dot_t(mat_bf16, vec_f32):
    hi = vec_f32.astype(jnp.bfloat16)
    lo = (vec_f32 - hi.astype(jnp.float32)).astype(jnp.bfloat16)
    dims = (((0,), (0,)), ((), ()))
    out = lax.dot_general(mat_bf16, hi, dims, preferred_element_type=jnp.float32)
    return out + lax.dot_general(mat_bf16, lo, dims, preferred_element_type=jnp.float32)


def prepare(tile):
    n = tile.shape[0]
    nb = n // BLOCK
    blocks = jnp.stack(
        [tile[j * BLOCK : (j + 1) * BLOCK, j * BLOCK : (j + 1) * BLOCK] for j in range(nb)]
    ).astype(jnp.float32)
    eye = jnp.eye(BLOCK, dtype=jnp.float32)
    diag = jnp.sum(blocks * eye[None], axis=2)
    lower = jnp.tril(jnp.ones((BLOCK, BLOCK), jnp.bool_), -1)
    nil = jnp.where(lower[None], blocks / diag[:, :, None], 0.0)
    prod = eye[None] - nil
    power = nil
    steps = 1
    while 2**steps < BLOCK:
        power = jnp.einsum("bij,bjk->bik", power, power, precision=HIGH)
        prod = jnp.einsum("bij,bjk->bik", prod, eye[None] + power, precision=HIGH)
        steps += 1
    return (prod, 1.0 / diag)


def apply_solve(tile, prod, inv_diag, rhs):
    n = tile.shape[0]
    nb = n // BLOCK
    cols = rhs.shape[1]

    def body(i, carry):
        rest, out = carry
        j = nb - 1 - i
        r_j = lax.dynamic_slice_in_dim(rest, j * BLOCK, BLOCK, 0)
        p_j = lax.dynamic_index_in_dim(prod, j, 0, keepdims=False)
        d_j = lax.dynamic_index_in_dim(inv_diag, j, 0, keepdims=False)
        v_j = jnp.einsum("ji,jk->ik", p_j, r_j, precision=HIGH) * d_j[:, None]
        rows = lax.dynamic_slice_in_dim(tile, j * BLOCK, BLOCK, 0)
        rest = rest - split_dot_t(rows, v_j)
        out = lax.dynamic_update_slice_in_dim(out, v_j, j * BLOCK, 0)
        return (rest, out)

    _, out = lax.fori_loop(0, nb, body, (rhs, jnp.zeros((n, cols), jnp.float32)))
    return out


def on_device(front, anc_weight, solved, owners, indices, counts, rhs_side):
    row_count = lax.axis_size("row")
    col_count = lax.axis_size("col")
    tiles_block = row_count * col_count
    row_index = lax.axis_index("row")
    col_index = lax.axis_index("col")
    tile_rows = indices.shape[1]
    columns = solved.shape[1]
    self_id = row_index * col_count + col_index
    owner_grid = owners.reshape(row_count, tiles_block)
    mine = (owner_grid == self_id).astype(jnp.int32)
    position = jnp.sum(mine * jnp.arange(tiles_block, dtype=jnp.int32)[None, :], axis=1)
    tile_ids = jnp.arange(row_count, dtype=jnp.int32) * tiles_block + position
    local_rows = indices[tile_ids]
    live_rows = jnp.arange(tile_rows, dtype=jnp.int32)[None, :] < counts[tile_ids][:, None]
    picked = solved[local_rows.reshape(-1)].reshape(row_count, tile_rows, columns)
    picked = jnp.where(live_rows[:, :, None], picked, jnp.zeros_like(picked))
    block_owners = lax.dynamic_slice_in_dim(owners, row_index * tiles_block, tiles_block)
    outgoing = jnp.broadcast_to(picked[:, None], (row_count, col_count, tile_rows, columns))
    outgoing = outgoing.reshape(row_count * col_count * tile_rows, columns)
    received = lax.all_to_all(outgoing, ("row", "col"), split_axis=0, concat_axis=0, tiled=True)
    slot_rows = received.reshape(tiles_block, tile_rows, columns)
    anc_values = slot_rows[block_owners].reshape(tiles_block * tile_rows, columns)
    weight_tile = lax.all_gather(anc_weight, "rhs", axis=0, tiled=True)
    front_tile = lax.all_gather(front, "rhs", axis=0, tiled=True)
    width = front_tile.shape[1]
    anc_total = lax.dot_general(
        weight_tile, anc_values, (((0,), (0,)), ((), ())), preferred_element_type=jnp.float32
    )
    prod, inv_diag = prepare(front_tile)
    rhs_values = rhs_side.astype(jnp.float32)
    down = [(1, 0)]
    left = [(1, 0)]
    right = [(0, 1)]
    own_one = anc_total.astype(jnp.bfloat16)
    other_one = lax.ppermute(own_one, "row", [(0, 1)])
    reduced_one = rhs_values - own_one.astype(jnp.float32) - other_one.astype(jnp.float32)
    sol_one = apply_solve(front_tile, prod, inv_diag, reduced_one).astype(jnp.bfloat16)
    got_one = lax.ppermute(sol_one, "col", left)
    sol_one = jnp.where(col_index == 1, sol_one, got_one)
    own_zero = (anc_total + split_dot_t(front_tile, sol_one.astype(jnp.float32))).astype(
        jnp.bfloat16
    )
    own_zero = jnp.where(row_index == 0, anc_total.astype(jnp.bfloat16), own_zero)
    other_zero = lax.ppermute(own_zero, "row", down)
    reduced_zero = rhs_values - own_zero.astype(jnp.float32) - other_zero.astype(jnp.float32)
    sol_zero = apply_solve(front_tile, prod, inv_diag, reduced_zero).astype(jnp.bfloat16)
    got_zero = lax.ppermute(sol_zero, "col", right)
    sol_zero = jnp.where(col_index == 0, sol_zero, got_zero)
    return jnp.where(row_index == 1, sol_one, sol_zero)


def solution(mesh):
    placed = (
        P(("row", "rhs"), "col"),
        P(("row", "rhs"), "col"),
        P(("row", "col"), "rhs"),
        P(),
        P(),
        P(),
        P("row", "rhs"),
    )
    return jax.shard_map(
        on_device, mesh=mesh, in_specs=placed, out_specs=P("row", "rhs"), check_vma=False
    )
```

profile of v0, /device:TPU:2, one launch (start us, length us, event | category | flops | bytes accessed | tf_op | source)
XLA Modules:
  0.0 487.1 jit_solution(5792975368108984710)
XLA Ops:
  13.2 5.5 %all-to-all-start = ((bf16[4,128,128]{2,1,0:T(8,128)(2,1)}), bf16[4,128,128]{2,1,0:T(8,128)(2,1)S(1)}, u32[]{:S(2)}, u32[]{:S(2)}) async-start(bf16[4,128,128]{2,1,0:T(8,128)(2,1)} %bitcast.9), calls=%async_computation | async-start | bytes 262144 | tf_op jit(solution)/shard_map/all_to_all | solution.py:79
  19.5 2.0 all-to-all-done
  22.1 109.4 %all-gather.3.cloned.1.call-done = bf16[512,2048]{1,0:T(8,128)(2,1)} async-done(((bf16[8,2048]{1,0:T(8,128)(2,1)}), bf16[512,2048]{1,0:T(8,128)(2,1)}) %all-gather.3.cloned.1.call-update) | async-done | bytes 2097168 | tf_op jit(solution)/shard_map/all_gather | solution.py:82
  131.5 2.1 fusion.80
  137.7 1.5 copy.12
  139.2 142.6 %all-gather.5.cloned.1.call-done = bf16[2048,2048]{1,0:T(8,128)(2,1)} async-done(((bf16[32,2048]{1,0:T(8,128)(2,1)}), bf16[2048,2048]{1,0:T(8,128)(2,1)}) %all-gather.5.cloned.1.call-update) | async-done | bytes 8388624 | tf_op jit(solution)/shard_map/all_gather | solution.py:83
  294.5 1.5 fusion.45
  308.1 2.2 fusion.85
  310.4 64.9 %while.34 = (s32[]{:T(128)}, f32[2048,128]{1,0:T(8,128)S(1)}, bf16[2048,128]{1,0:T(8,128)(2,1)S(1)}, bf16[2048,2048]{1,0:T(8,128)(2,1)}, f32[16,128,128]{2,1,0:T...) while((s32[]{:T(128)}, f32[2048,128]{1,0:T(8,128)S(1)}, ...), condition=%wide.region_3.4_spmd, body=%wide.region_2.3_spmd.sunk | while | flops 160006144 | bytes 5639389 | solution.py:55
  313.0 1.5 fusion.124
  317.0 1.5 fusion.124
  321.1 1.5 fusion.124
  325.1 1.5 fusion.124
  333.2 1.5 fusion.124
  341.4 1.5 fusion.124
  349.5 1.5 fusion.124
  357.6 1.5 fusion.124
  365.7 1.5 fusion.124
  373.8 1.5 fusion.124
  375.3 3.4 collective-permute-start.1
  378.7 8.0 %collective-permute-done.1 = bf16[2048,128]{1,0:T(8,128)(2,1)S(1)} collective-permute-done((bf16[2048,128]{1,0:T(8,128)(2,1)S(1)}, bf16[2048,128]{1,0:T(8,128)(2,1)S(1)}, u32[]{:S(2)}, u32[]{:S(2)}) %collective-permute-start.1) | collective-permute-done | bytes 524320 | tf_op jit(solution)/shard_map/ppermute | solution.py:97
  386.8 4.8 fusion.48
  394.3 2.5 collective-permute-done.2
  398.4 64.9 %while.35 = (s32[]{:T(128)}, f32[2048,128]{1,0:T(8,128)S(1)}, bf16[2048,128]{1,0:T(8,128)(2,1)S(1)}, bf16[2048,2048]{1,0:T(8,128)(2,1)}, f32[16,128,128]{2,1,0:T...) while((s32[]{:T(128)}, f32[2048,128]{1,0:T(8,128)S(1)}, ...), condition=%wide.region_5.6_spmd, body=%wide.region_4.5_spmd.sunk | while | flops 160006144 | bytes 5639389 | solution.py:55
  405.1 1.5 fusion.130
  409.1 1.5 fusion.130
  413.2 1.5 fusion.130
  417.2 1.5 fusion.130
  425.4 1.5 fusion.130
  437.5 1.5 fusion.130
  449.7 1.5 fusion.130
  464.7 14.7 %collective-permute-done.3 = bf16[2048,128]{1,0:T(8,128)(2,1)S(1)} collective-permute-done((bf16[2048,128]{1,0:T(8,128)(2,1)S(1)}, bf16[2048,128]{1,0:T(8,128)(2,1)S(1)}, u32[]{:S(2)}, u32[]{:S(2)}) %collective-permute-start.3) | collective-permute-done | bytes 524320 | tf_op jit(solution)/shard_map/ppermute | solution.py:106
  (184 shorter events, 146.4 us)
Async XLA Ops:
  6.5 4.9 %copy-start = (bf16[512,128]{1,0:T(8,128)(2,1)S(1)}, bf16[512,128]{1,0:T(8,128)(2,1)}, u32[]{:S(2)}) copy-start(bf16[512,128]{1,0:T(8,128)(2,1)} %param.13) | copy-start | bytes 393220
  6.5 125.0 %all-gather.3.cloned.1.call-start = ((), (), s32[]{:S(2)}) async-start(), calls=%async_computation.1 | async-start | bytes 2129920 | tf_op jit(solution)/shard_map/all_gather | solution.py:82
  7.3 274.6 %all-gather.5.cloned.1.call-start = ((), (), s32[]{:S(2)}) async-start(), calls=%async_computation.2 | async-start | bytes 8519680 | tf_op jit(solution)/shard_map/all_gather | solution.py:83
  13.2 8.3 %all-to-all-start = ((bf16[4,128,128]{2,1,0:T(8,128)(2,1)}), bf16[4,128,128]{2,1,0:T(8,128)(2,1)S(1)}, u32[]{:S(2)}, u32[]{:S(2)}) async-start(bf16[4,128,128]{2,1,0:T(8,128)(2,1)} %bitcast.9), calls=%async_computation | async-start | bytes 262144 | tf_op jit(solution)/shard_map/all_to_all | solution.py:79
  133.6 2.8 collective-permute-start
  375.3 11.4 %collective-permute-start.1 = (bf16[2048,128]{1,0:T(8,128)(2,1)S(1)}, bf16[2048,128]{1,0:T(8,128)(2,1)S(1)}, u32[]{:S(2)}, u32[]{:S(2)}) collective-permute-start(bf16[2048,128]{1,0:T(8,128)(2,1)S(1)} %get-tuple-element.313), channel_id=1, source_target_pairs={{64,0},{65,1},{66,2},{67,3},{68,4},{69,5},{70,6},{71,7},{72,8},{73... | collective-permute-start | bytes 1572872 | tf_op jit(solution)/shard_map/ppermute | solution.py:97
  378.7 12.9 %slice-start = ((s8[8388608]{0:T(1024)(128)(4,1)}), s8[4194304]{0:T(1024)(128)(4,1)S(1)}, s32[]{:S(2)}) async-start(s8[8388608]{0:T(1024)(128)(4,1)} %bitcast.128), calls=%async_computation.3 | async-start | bytes 8388608
  386.8 4.8 slice-start.1
  393.0 1.3 copy-start.1
  393.0 3.8 collective-permute-start.2
  463.4 16.0 %collective-permute-start.3 = (bf16[2048,128]{1,0:T(8,128)(2,1)S(1)}, bf16[2048,128]{1,0:T(8,128)(2,1)S(1)}, u32[]{:S(2)}, u32[]{:S(2)}) collective-permute-start(bf16[2048,128]{1,0:T(8,128)(2,1)S(1)} %get-tuple-element.314), channel_id=1, source_target_pairs={{0,64},{1,65},{2,66},{3,67},{4,68},{5,69},{6,70},{7,71},{8,72},{9,... | collective-permute-start | bytes 1572872 | tf_op jit(solution)/shard_map/ppermute | solution.py:106
Sparse Core Ops, SparseCore 0:
  10.9 120.5 all-gather.2
  135.0 146.8 all-gather.4
where the time goes:
time: 493 us; the launch traced here: 487 us
  waiting for transfers between devices  281 us (57%)
  matrix products  152 us (31%)
  local copies, waits for them, and re-layouts  20.6 us (4%)
  between operations  13.7 us (3%)
  starting transfers between devices  12.9 us (3%)
  other arithmetic  5.61 us (1%)
    all_gather x1, waiting for transfers between devices, on_device(): front_tile = lax.all_gather(front, 'rhs', axis=0, tiled=True)  143 us
    all_gather x1, waiting for transfers between devices, on_device(): weight_tile = lax.all_gather(anc_weight, 'rhs', axis=0, tiled=True)  109 us
    dot_general x33, matrix products, split_dot_t(): lax.dot_general(mat_bf16, lo, dims, preferred_element_type=jnp.float32)  51.9 us
    dot_general x33, matrix products, split_dot_t(): lax.dot_general(mat_bf16, hi, dims, preferred_element_type=jnp.float32)  45.5 us
    dot_general x32, matrix products, body(): v_j = jnp.einsum('ji,jk->ik', p_j, r_j, precision=HIGH) * d_j[:, None]  36.7 us
    ppermute x1, waiting for transfers between devices, on_device(): got_zero = lax.ppermute(sol_zero, 'col', right)  14.7 us
    unnamed x24, local copies, waits for them, and re-layouts  12.7 us
  transfers between devices with their start and end apart: 7, of which 7 were waited for; matrix products, arithmetic and copies ran while one was open for 3% of the time, Pallas kernels for 0%

commit v1 on v0

--- a/solution.py
+++ b/solution.py
@@ -80,7 +80,9 @@
     slot_rows = received.reshape(tiles_block, tile_rows, columns)
     anc_values = slot_rows[block_owners].reshape(tiles_block * tile_rows, columns)
     weight_tile = lax.all_gather(anc_weight, "rhs", axis=0, tiled=True)
-    front_tile = lax.all_gather(front, "rhs", axis=0, tiled=True)
+    front_tile = jnp.concatenate(
+        lax.all_to_all(jnp.stack([front] * lax.axis_size("rhs")), "rhs", 0, 0), axis=0
+    )
     width = front_tile.shape[1]
     anc_total = lax.dot_general(
         weight_tile, anc_values, (((0,), (0,)), ((), ())), preferred_element_type=jnp.float32

time: 493 us -> 450 us (0.913)
  waiting for transfers between devices: 281 us -> 214 us
  starting transfers between devices: 12.9 us -> 20.7 us
  blocking collectives: 0 us -> 7.4 us
    all_gather x1 -> x0, waiting for transfers between devices: 143 us -> none  [on_device(): front_tile = lax.all_gather(front, 'rhs', axis=0, tiled=True)]
    all_gather x1, waiting for transfers between devices: 109 us -> 168 us  [on_device(): weight_tile = lax.all_gather(anc_weight, 'rhs', axis=0, tiled=True)]
    all_to_all x1, waiting for transfers between devices: 2.04 us -> 18.6 us  [on_device(): lax.all_to_all(jnp.stack([front] * lax.axis_size('rhs')), 'rhs', 0, 0)]
    all_to_all x0 -> x1, blocking collectives: none -> 7.4 us  [on_device(): lax.all_to_all(outgoing, ('row', 'col'), split_axis=0, concat_axis=0, til...]
    all_to_all x1, starting transfers between devices: 5.53 us -> 12.6 us  [on_device(): lax.all_to_all(jnp.stack([front] * lax.axis_size('rhs')), 'rhs', 0, 0)]
    another operation x2 -> x3, local copies, waits for them, and re-layouts: 0.14 us -> 5.34 us  [the longest x1 5.2 us: on_device(): jnp.stack([front] * lax.axis_size('rhs'))]
  transfers between devices with their start and end apart: 7 -> 6, of which waited for: 7 -> 6; matrix products, arithmetic and copies ran while one was open for 3% -> 1% of each run, Pallas kernels for 0% -> 0%
where the time goes in v1:
time: 450 us; the launch traced here: 442 us
  waiting for transfers between devices  214 us (48%)
  matrix products  155 us (34%)
  local copies, waits for them, and re-layouts  24.1 us (5%)
  starting transfers between devices  20.7 us (5%)
  between operations  13.7 us (3%)
  blocking collectives  7.4 us (2%)
  other arithmetic  4.92 us (1%)
    all_gather x1, waiting for transfers between devices, on_device(): weight_tile = lax.all_gather(anc_weight, 'rhs', axis=0, tiled=True)  168 us
    dot_general x33, matrix products, split_dot_t(): lax.dot_general(mat_bf16, lo, dims, preferred_element_type=jnp.float32)  51.7 us
    dot_general x33, matrix products, split_dot_t(): lax.dot_general(mat_bf16, hi, dims, preferred_element_type=jnp.float32)  48.9 us
    dot_general x32, matrix products, body(): v_j = jnp.einsum('ji,jk->ik', p_j, r_j, precision=HIGH) * d_j[:, None]  36.7 us
    all_to_all x1, waiting for transfers between devices, on_device(): lax.all_to_all(jnp.stack([front] * lax.axis_size('rhs')), 'rhs', 0, 0)  18.6 us
    ppermute x1, waiting for transfers between devices, on_device(): got_zero = lax.ppermute(sol_zero, 'col', right)  14.7 us
    all_to_all x1, starting transfers between devices, on_device(): lax.all_to_all(jnp.stack([front] * lax.axis_size('rhs')), 'rhs', 0, 0)  12.6 us
    unnamed x24, local copies, waits for them, and re-layouts  11.7 us
  transfers between devices with their start and end apart: 6, of which 6 were waited for; matrix products, arithmetic and copies ran while one was open for 1% of the time, Pallas kernels for 0%

profile of v1, /device:TPU:2, one launch (start us, length us, event | category | flops | bytes accessed | tf_op | source)
XLA Modules:
  0.0 441.7 jit_solution(5581959899953794531)
XLA Ops:
  11.1 7.4 %all_to_all.14 = bf16[4,128,128]{2,1,0:T(8,128)(2,1)S(1)} all-to-all(bf16[4,128,128]{2,1,0:T(8,128)(2,1)S(1)} %bitcast.130), channel_id=1, replica_groups=mesh['row'=2,'col'=2,'rhs'=64] {'row','col'}, dimensions={0} | all-to-all | bytes 262144 | tf_op jit(solution)/shard_map/all_to_all | solution.py:79
  18.5 5.2 %stack.36 = bf16[64,32,2048]{2,1,0:T(8,128)(2,1)} broadcast(bf16[32,2048]{1,0:T(8,128)(2,1)} %param.11), dimensions={1,2} | broadcast | bytes 8519680 | tf_op jit(solution)/shard_map/stack | solution.py:84
  23.7 12.6 %all-to-all-start.1 = ((bf16[64,32,2048]{2,1,0:T(8,128)(2,1)}), bf16[64,32,2048]{2,1,0:T(8,128)(2,1)}, u32[]{:S(2)}, u32[]{:S(2)}) async-start(bf16[64,32,2048]{2,1,0:T(8,128)(2,1)} %stack.36), calls=%async_computation.1 | async-start | bytes 16777216 | tf_op jit(solution)/shard_map/all_to_all | solution.py:84
  37.8 168.4 %all-gather.2.cloned.1.call-done = bf16[512,2048]{1,0:T(8,128)(2,1)} async-done(((bf16[8,2048]{1,0:T(8,128)(2,1)}), bf16[512,2048]{1,0:T(8,128)(2,1)}) %all-gather.2.cloned.1.call-update) | async-done | bytes 2097168 | tf_op jit(solution)/shard_map/all_gather | solution.py:82
  206.1 2.1 fusion.80
  208.3 1.5 collective-permute-start
  212.2 1.5 copy.12
  213.8 18.6 %all-to-all-done.1 = bf16[64,32,2048]{2,1,0:T(8,128)(2,1)} async-done(((bf16[64,32,2048]{2,1,0:T(8,128)(2,1)}), bf16[64,32,2048]{2,1,0:T(8,128)(2,1)}, u32[]{:S(2)}, u32[]{:S(2)}) %all-to-all-start.1) | async-done | bytes 8388640 | tf_op jit(solution)/shard_map/all_to_all | solution.py:84
  245.0 1.5 fusion.45
  258.7 2.2 fusion.85
  261.0 64.9 %while.34 = (s32[]{:T(128)}, f32[2048,128]{1,0:T(8,128)S(1)}, bf16[2048,128]{1,0:T(8,128)(2,1)S(1)}, bf16[2048,2048]{1,0:T(8,128)(2,1)}, f32[16,128,128]{2,1,0:T...) while((s32[]{:T(128)}, f32[2048,128]{1,0:T(8,128)S(1)}, ...), condition=%wide.region_3.4_spmd, body=%wide.region_2.3_spmd.sunk | while | flops 160006144 | bytes 5639389 | solution.py:55
  263.6 1.5 fusion.124
  267.6 1.5 fusion.124
  271.7 1.5 fusion.124
  275.7 1.5 fusion.124
  279.8 1.5 fusion.124
  283.8 1.5 fusion.124
  287.9 1.5 fusion.124
  292.0 1.5 fusion.124
  296.0 1.5 fusion.124
  300.1 1.5 fusion.124
  304.1 1.5 fusion.124
  312.2 1.5 fusion.124
  320.3 1.5 fusion.124
  325.9 4.0 collective-permute-start.1
  329.8 8.4 %collective-permute-done.1 = bf16[2048,128]{1,0:T(8,128)(2,1)S(1)} collective-permute-done((bf16[2048,128]{1,0:T(8,128)(2,1)S(1)}, bf16[2048,128]{1,0:T(8,128)(2,1)S(1)}, u32[]{:S(2)}, u32[]{:S(2)}) %collective-permute-start.1) | collective-permute-done | bytes 524320 | tf_op jit(solution)/shard_map/ppermute | solution.py:99
  338.3 4.7 %fusion.48 = f32[128,2048]{1,0:T(8,128)S(1)} fusion(bf16[2048,2048]{1,0:T(8,128)(2,1)} %bitcast.12, bf16[2048,128]{1,0:T(8,128)(2,1)S(1)} %broadcast_select_fusion), kind=kOutput, calls=%fused_computation.67 | convolution fusion | flops 1074528256 | bytes 9961472 | tf_op jit(solution)/shard_map/dot_general | solution.py:15
  343.0 4.7 %fusion.29 = bf16[2048,128]{0,1:T(8,128)(2,1)S(1)} fusion(f32[128,2048]{1,0:T(8,128)S(1)} %fusion.80, f32[128,2048]{1,0:T(8,128)S(1)} %fusion.48, bf16[2048,128]{1,0:T(8,128)(2,1)S(1)} %broadcast_select_fusion, bf16[2048,2048]{1,0:T(8,128)(2,1)} %bitcast.12, pred[]{:T(512)S(6)} %eq.49), kind=kOutput, calls=%fused_computation.44 | convolution fusion | flops 1075052544 | bytes 11534337 | tf_op jit(solution)/shard_map/dot_general | solution.py:14
  349.0 2.5 collective-permute-done.2
  353.2 64.8 %while.35 = (s32[]{:T(128)}, f32[2048,128]{1,0:T(8,128)S(1)}, bf16[2048,128]{1,0:T(8,128)(2,1)S(1)}, bf16[2048,2048]{1,0:T(8,128)(2,1)}, f32[16,128,128]{2,1,0:T...) while((s32[]{:T(128)}, f32[2048,128]{1,0:T(8,128)S(1)}, ...), condition=%wide.region_5.6_spmd, body=%wide.region_4.5_spmd.sunk | while | flops 160006144 | bytes 5639389 | solution.py:55
  355.7 1.5 fusion.130
  419.3 14.7 %collective-permute-done.3 = bf16[2048,128]{1,0:T(8,128)(2,1)S(1)} collective-permute-done((bf16[2048,128]{1,0:T(8,128)(2,1)S(1)}, bf16[2048,128]{1,0:T(8,128)(2,1)S(1)}, u32[]{:S(2)}, u32[]{:S(2)}) %collective-permute-start.3) | collective-permute-done | bytes 524320 | tf_op jit(solution)/shard_map/ppermute | solution.py:108
  (182 shorter events, 145.8 us)
Async XLA Ops:
  6.5 3.6 copy-start
  23.7 13.4 %copy-start.3 = (s32[8]{0:T(128)S(1)}, s32[8]{0:T(128)}, u32[]{:S(2)}) copy-start(s32[8]{0:T(128)} %param.14) | copy-start | bytes 100
  23.7 186.1 %copy-start.2 = (bf16[2048,128]{1,0:T(8,128)(2,1)S(1)}, bf16[2048,128]{1,0:T(8,128)(2,1)}, u32[]{:S(2)}) copy-start(bf16[2048,128]{1,0:T(8,128)(2,1)} %param.17) | copy-start | bytes 1572868
  23.7 208.7 %all-to-all-start.1 = ((bf16[64,32,2048]{2,1,0:T(8,128)(2,1)}), bf16[64,32,2048]{2,1,0:T(8,128)(2,1)}, u32[]{:S(2)}, u32[]{:S(2)}) async-start(bf16[64,32,2048]{2,1,0:T(8,128)(2,1)} %stack.36), calls=%async_computation.1 | async-start | bytes 16777216 | tf_op jit(solution)/shard_map/all_to_all | solution.py:84
  36.4 169.8 %all-gather.2.cloned.1.call-start = ((), (), s32[]{:S(2)}) async-start(), calls=%async_computation.2 | async-start | bytes 2129920 | tf_op jit(solution)/shard_map/all_gather | solution.py:82
  208.3 2.8 collective-permute-start
  325.9 12.4 %collective-permute-start.1 = (bf16[2048,128]{1,0:T(8,128)(2,1)S(1)}, bf16[2048,128]{1,0:T(8,128)(2,1)S(1)}, u32[]{:S(2)}, u32[]{:S(2)}) collective-permute-start(bf16[2048,128]{1,0:T(8,128)(2,1)S(1)} %get-tuple-element.313), channel_id=1, source_target_pairs={{64,0},{65,1},{66,2},{67,3},{68,4},{69,5},{70,6},{71,7},{72,8},{73... | collective-permute-start | bytes 1572872 | tf_op jit(solution)/shard_map/ppermute | solution.py:99
  347.7 1.3 copy-start.1
  347.7 3.8 collective-permute-start.2
  418.0 16.0 %collective-permute-start.3 = (bf16[2048,128]{1,0:T(8,128)(2,1)S(1)}, bf16[2048,128]{1,0:T(8,128)(2,1)S(1)}, u32[]{:S(2)}, u32[]{:S(2)}) collective-permute-start(bf16[2048,128]{1,0:T(8,128)(2,1)S(1)} %get-tuple-element.314), channel_id=1, source_target_pairs={{0,64},{1,65},{2,66},{3,67},{4,68},{5,69},{6,70},{7,71},{8,72},{9,... | collective-permute-start | bytes 1572872 | tf_op jit(solution)/shard_map/ppermute | solution.py:108
Sparse Core Ops, SparseCore 0:
  40.7 165.3 all-gather.1
